TPU v7x, 32 devices: a whole 2x2x4 slice. The times are simulated.
32 devices in a mesh: rec: 2 (over core), space: 16 (over z, y, x).
Axes of the slice: x: 2, y: 2, z: 4, core: 2. Of those that a mesh axis runs over, the one named last changes fastest.
Arguments:
- footprints: bfloat16 [32, 120, 8400], P(('rec', 'space')), may hold values from 0 to 1
- time_cov: bfloat16 [120, 120], replicated, may hold values from -1 to 3
- lat_cov: bfloat16 [70, 70], replicated, may hold values from -1 to 3
- lon_cov: bfloat16 [120, 120], replicated, may hold values from -1 to 3
Outputs:
- gram: float32 [32, 32], P(('rec', 'space'))
All inputs are finite; a program needn't handle non-finite values.
Results may differ from a plain program's by a relative error of at most 0.0003.
Values may be sent and summed in bfloat16 or wider, within the bound.
No kernel may reach another device: no remote copies, remote signals or barrier semaphores. Data moves between devices by JAX's collectives and lax.ppermute only.
A program may use at most 64 MiB of HBM per device.

v0:
```python
import jax
import jax.numpy as jnp
from jax import lax
from jax.sharding import PartitionSpec as P


def weigh_footprints(footprints, time_cov, lat_cov, lon_cov):
    receptors_here, time_count, cell_count = footprints.shape
    lat_count = lat_cov.shape[0]
    lon_count = lon_cov.shape[0]
    along_lon = jnp.dot(
        footprints.reshape(receptors_here * time_count * lat_count, lon_count),
        lon_cov,
        preferred_element_type=jnp.float32,
    ).astype(jnp.bfloat16)
    along_lat = jnp.einsum(
        "rab,ac->rcb",
        along_lon.reshape(receptors_here * time_count, lat_count, lon_count),
        lat_cov,
        preferred_element_type=jnp.float32,
    ).astype(jnp.bfloat16)
    return jnp.einsum(
        "rtc,ts->rsc",
        along_lat.reshape(receptors_here, time_count, cell_count),
        time_cov,
        preferred_element_type=jnp.float32,
    ).astype(jnp.bfloat16)


def flatten_padded(values, devices):
    receptors_here = values.shape[0]
    flat = values.reshape(receptors_here, -1)
    length = flat.shape[1]
    per_device = -(-length // devices)
    per_device = -(-per_device // 128) * 128
    return jnp.pad(flat, ((0, 0), (0, per_device * devices - length)))


def regroup(values):
    moved = (
        lax.all_to_all(
            lax.all_to_all(values[0], "space", split_axis=1, concat_axis=0, tiled=True),
            "rec",
            split_axis=1,
            concat_axis=0,
            tiled=True,
        ),
        lax.all_to_all(
            lax.all_to_all(values[1], "space", split_axis=1, concat_axis=0, tiled=True),
            "rec",
            split_axis=1,
            concat_axis=0,
            tiled=True,
        ),
    )
    return moved


def local(footprints, time_cov, lat_cov, lon_cov):
    rec_count = lax.axis_size("rec")
    space_count = lax.axis_size("space")
    devices = rec_count * space_count
    plain = flatten_padded(footprints, devices)
    weighted = flatten_padded(weigh_footprints(footprints, time_cov, lat_cov, lon_cov), devices)
    weighted_all, plain_all = regroup((weighted, plain))
    partial_value = lax.dot_general(
        weighted_all, plain_all, (((1,), (1,)), ((), ())), preferred_element_type=jnp.float32
    )
    return lax.psum_scatter(partial_value, ("rec", "space"), scatter_dimension=0, tiled=True)


def solution(mesh):
    in_specs = (P(("rec", "space"), None, None), P(), P(), P())
    out_specs = P(("rec", "space"), None)
    return jax.shard_map(local, mesh=mesh, in_specs=in_specs, out_specs=out_specs, check_vma=False)
```

profile of v0, /device:TPU:0, one launch (start us, length us, event | category | flops | bytes accessed | tf_op | source)
XLA Modules:
  0.0 254.2 jit_solution(8349191223248169489)
XLA Ops:
  0.0 5.8 %reshape.41 = bf16[8400,120]{1,0:T(8,128)(2,1)S(1)} reshape(bf16[1,120,8400]{2,1,0:T(8,128)(2,1)} %param.4) | data formatting | bytes 4032000 | tf_op jit(solution)/shard_map/reshape | solution.py:12
  5.9 2.1 convolution_convert_fusion.1
  7.9 4.1 %copy.15 = bf16[8400,120]{1,0:T(8,128)(2,1)} copy(bf16[8400,120]{0,1:T(8,128)(2,1)} %convolution_convert_fusion.1) | data formatting | bytes 4032000 | tf_op jit(solution)/shard_map/convert_element_type | solution.py:15
  12.0 2.8 %reshape.42 = bf16[120,70,120]{2,1,0:T(8,128)(2,1)S(1)} reshape(bf16[8400,120]{1,0:T(8,128)(2,1)} %copy.15) | data formatting | bytes 4032000 | tf_op jit(solution)/shard_map/reshape | solution.py:18
  14.8 2.2 convert_bitcast_fusion
  17.0 3.6 %copy.17 = bf16[120,70,120]{0,2,1:T(8,128)(2,1)S(1)} copy(bf16[120,70,120]{2,1,0:T(8,128)(2,1)} %convert_bitcast_fusion) | data formatting | bytes 4032000 | tf_op jit(solution)/shard_map/convert_element_type | solution.py:21
  20.6 2.1 fusion
  22.7 4.7 %reshape.49 = bf16[1008000]{0:T(1024)(128)(2,1)S(1)} reshape(bf16[120,8400]{1,0:T(8,128)(2,1)} %fusion) | data formatting | bytes 4032000
  27.4 23.2 %reshape.44 = bf16[1,1008000]{1,0:T(2,128)(2,1)S(1)} reshape(bf16[1008000]{0:T(1024)(128)(2,1)S(1)} %reshape.49) | data formatting | bytes 4032000 | tf_op jit(solution)/shard_map/reshape | solution.py:32
  50.6 5.9 %pad.7 = bf16[1,1011712]{1,0:T(2,128)(2,1)} pad(bf16[1,1008000]{1,0:T(2,128)(2,1)S(1)} %reshape.44, bf16[]{:T(256)} %constant.2.clone.1), padding=0_0x0_3712 | pad | bytes 4039426 | tf_op jit(solution)/shard_map/jit(_pad)/pad | solution.py:36
  56.5 0.5 broadcast.6
  57.0 12.8 %reduce.4 = bf16[16,63232]{1,0:T(8,128)(2,1)S(1)} reduce(bf16[16,1,63232]{2,1,0:T(2,128)(2,1)} %bitcast.37, bf16[]{:T(256)} %broadcast.6), dimensions={1}, to_apply=%bitcast.22.reduce_sub_computation | reduce | bytes 4046850
  69.8 1.6 reshape.53
  71.4 8.5 %all-to-all-start = ((bf16[16,2,31616]{2,1,0:T(2,128)(2,1)}), bf16[16,2,31616]{2,1,0:T(2,128)(2,1)}, u32[]{:S(2)}, u32[]{:S(2)}) async-start(bf16[16,2,31616]{2,1,0:T(2,128)(2,1)} %reshape.53), calls=%async_computation | async-start | bytes 4046848 | tf_op jit(solution)/shard_map/all_to_all | solution.py:42
  79.9 5.0 %reshape.51 = bf16[1008000]{0:T(1024)(128)(2,1)} reshape(bf16[1,120,8400]{2,1,0:T(8,128)(2,1)S(1)} %copy-done.2) | data formatting | bytes 4032000
  84.9 20.0 %reshape.45 = bf16[1,1008000]{1,0:T(2,128)(2,1)S(1)} reshape(bf16[1008000]{0:T(1024)(128)(2,1)} %reshape.51) | data formatting | bytes 4032000 | tf_op jit(solution)/shard_map/reshape | solution.py:32
  104.8 5.9 %pad.8 = bf16[1,1011712]{1,0:T(2,128)(2,1)} pad(bf16[1,1008000]{1,0:T(2,128)(2,1)S(1)} %reshape.45, bf16[]{:T(256)} %constant.2.clone.1), padding=0_0x0_3712 | pad | bytes 4039426 | tf_op jit(solution)/shard_map/jit(_pad)/pad | solution.py:36
  110.7 12.8 %reduce.5 = bf16[16,63232]{1,0:T(8,128)(2,1)S(1)} reduce(bf16[16,1,63232]{2,1,0:T(2,128)(2,1)} %bitcast.38, bf16[]{:T(256)} %broadcast.6), dimensions={1}, to_apply=%bitcast.24.reduce_sub_computation | reduce | bytes 4046850
  123.5 1.6 reshape.55
  125.2 6.8 %all-to-all-start.2 = ((bf16[16,2,31616]{2,1,0:T(2,128)(2,1)}), bf16[16,2,31616]{2,1,0:T(2,128)(2,1)S(1)}, u32[]{:S(2)}, u32[]{:S(2)}) async-start(bf16[16,2,31616]{2,1,0:T(2,128)(2,1)} %reshape.55), calls=%async_computation.2 | async-start | bytes 4046848 | tf_op jit(solution)/shard_map/all_to_all | solution.py:49
  132.0 12.4 %reshape.54 = bf16[16,1,63232]{2,1,0:T(2,128)(2,1)} reshape(bf16[16,2,31616]{2,1,0:T(2,128)(2,1)} %all-to-all-done) | data formatting | bytes 4046848
  144.4 13.2 %bitcast_reduce_fusion.1 = bf16[16,63232]{1,0:T(8,128)(2,1)S(1)} fusion(bf16[16,1,63232]{2,1,0:T(2,128)(2,1)} %reshape.54), kind=kLoop, calls=%fused_computation.9 | loop fusion | bytes 4046848 | tf_op jit(solution)/shard_map/all_to_all | solution.py:42
  157.6 1.5 copy.27
  159.0 14.5 %all-to-all-done.2 = bf16[16,2,31616]{2,1,0:T(2,128)(2,1)S(1)} async-done(((bf16[16,2,31616]{2,1,0:T(2,128)(2,1)}), bf16[16,2,31616]{2,1,0:T(2,128)(2,1)S(1)}, u32[]{:S(2)}, u32[]{:S(2)}) %all-to-all-start.2) | async-done | bytes 2023456 | tf_op jit(solution)/shard_map/all_to_all | solution.py:49
  173.6 5.0 %all-to-all-start.1 = ((bf16[16,2,31616]{2,0,1:T(8,128)(2,1)}), bf16[16,2,31616]{2,0,1:T(8,128)(2,1)}, u32[]{:S(2)}, u32[]{:S(2)}) async-start(bf16[16,2,31616]{2,0,1:T(8,128)(2,1)} %bitcast.42), calls=%async_computation.1 | async-start | bytes 4046848 | tf_op jit(solution)/shard_map/all_to_all | solution.py:41
  178.6 9.0 %reshape.56 = bf16[16,1,63232]{2,1,0:T(2,128)(2,1)} reshape(bf16[16,2,31616]{2,1,0:T(2,128)(2,1)S(1)} %all-to-all-done.2) | data formatting | bytes 4046848
  187.6 13.2 %bitcast_reduce_fusion = bf16[16,63232]{1,0:T(8,128)(2,1)S(1)} fusion(bf16[16,1,63232]{2,1,0:T(2,128)(2,1)} %reshape.56), kind=kLoop, calls=%fused_computation.8 | loop fusion | bytes 4046848 | tf_op jit(solution)/shard_map/all_to_all | solution.py:49
  200.8 0.1 copy.26
  200.9 5.4 %all_to_all.64 = bf16[16,2,31616]{2,0,1:T(8,128)(2,1)S(1)} all-to-all(bf16[16,2,31616]{2,0,1:T(8,128)(2,1)S(1)} %bitcast.43), channel_id=1, replica_groups=mesh['rec'=2,'space'=16] {'rec'}, dimensions={1} | all-to-all | bytes 4046848 | tf_op jit(solution)/shard_map/all_to_all | solution.py:48
  206.3 2.3 fusion.2
  208.7 45.1 %all-reduce.2 = f32[32,32]{1,0:T(8,128)S(1)} all-reduce(f32[32,32]{1,0:T(8,128)S(1)} %fusion.2), channel_id=2, replica_groups=mesh['rec'=2,'space'=16] {'rec','space'}, use_global_device_ids=true, to_apply=%region_0.1.clone | all-reduce | flops 1024 | bytes 8192
  253.7 0.5 constant_dynamic-slice_fusion
  (12 shorter events, 0.0 us)
Async XLA Ops:
  0.0 5.8 %copy-start = (bf16[120,120]{1,0:T(8,128)(2,1)S(1)}, bf16[120,120]{1,0:T(8,128)(2,1)}, u32[]{:S(2)}) copy-start(bf16[120,120]{1,0:T(8,128)(2,1)} %param.7) | copy-start | bytes 86404
  12.0 2.8 %copy-start.4 = (bf16[70,70]{1,0:T(8,128)(2,1)S(1)}, bf16[70,70]{1,0:T(8,128)(2,1)}, u32[]{:S(2)}) copy-start(bf16[70,70]{1,0:T(8,128)(2,1)} %param.6) | copy-start | bytes 29404
  17.0 3.6 %copy-start.3 = (bf16[120,120]{1,0:T(8,128)(2,1)S(1)}, bf16[120,120]{1,0:T(8,128)(2,1)}, u32[]{:S(2)}) copy-start(bf16[120,120]{1,0:T(8,128)(2,1)} %param.5) | copy-start | bytes 86404
  71.4 8.5 %copy-start.2 = (bf16[1,120,8400]{2,1,0:T(8,128)(2,1)S(1)}, bf16[1,120,8400]{2,1,0:T(8,128)(2,1)}, u32[]{:S(2)}) copy-start(bf16[1,120,8400]{2,1,0:T(8,128)(2,1)} %param.4) | copy-start | bytes 6048004
  71.4 53.8 %all-to-all-start = ((bf16[16,2,31616]{2,1,0:T(2,128)(2,1)}), bf16[16,2,31616]{2,1,0:T(2,128)(2,1)}, u32[]{:S(2)}, u32[]{:S(2)}) async-start(bf16[16,2,31616]{2,1,0:T(2,128)(2,1)} %reshape.53), calls=%async_computation | async-start | bytes 4046848 | tf_op jit(solution)/shard_map/all_to_all | solution.py:42
  125.2 48.4 %all-to-all-start.2 = ((bf16[16,2,31616]{2,1,0:T(2,128)(2,1)}), bf16[16,2,31616]{2,1,0:T(2,128)(2,1)S(1)}, u32[]{:S(2)}, u32[]{:S(2)}) async-start(bf16[16,2,31616]{2,1,0:T(2,128)(2,1)} %reshape.55), calls=%async_computation.2 | async-start | bytes 4046848 | tf_op jit(solution)/shard_map/all_to_all | solution.py:49
  173.6 27.4 %all-to-all-start.1 = ((bf16[16,2,31616]{2,0,1:T(8,128)(2,1)}), bf16[16,2,31616]{2,0,1:T(8,128)(2,1)}, u32[]{:S(2)}, u32[]{:S(2)}) async-start(bf16[16,2,31616]{2,0,1:T(8,128)(2,1)} %bitcast.42), calls=%async_computation.1 | async-start | bytes 4046848 | tf_op jit(solution)/shard_map/all_to_all | solution.py:41
  206.3 47.9 %copy-start.1 = (bf16[120,120]{1,0:T(8,128)(2,1)S(1)}, bf16[120,120]{1,0:T(8,128)(2,1)}, u32[]{:S(2)}) copy-start(bf16[120,120]{1,0:T(8,128)(2,1)} %param.7) | copy-start | bytes 86404
where the time goes:
time: 255 us; the launch traced here: 254 us
  local copies, waits for them, and re-layouts  134 us (53%)
  blocking collectives  50.4 us (20%)
  other arithmetic  25.6 us (10%)
  starting transfers between devices  20.4 us (8%)
  waiting for transfers between devices  14.5 us (6%)
  matrix products  8.68 us (3%)
    unnamed x1, blocking collectives  45.1 us
    reshape x2, local copies, waits for them, and re-layouts, flatten_padded(): flat = values.reshape(receptors_here, -1)  43.2 us
    unnamed x18, local copies, waits for them, and re-layouts  35.3 us
    unnamed x2, other arithmetic  25.6 us
    all_to_all x1, waiting for transfers between devices, regroup(): lax.all_to_all(values[1], 'space', split_axis=1, concat_axis=0, tiled=True)  14.5 us
    all_to_all x1, local copies, waits for them, and re-layouts, regroup(): lax.all_to_all(values[0], 'space', split_axis=1, concat_axis=0, tiled=True)  13.2 us
    all_to_all x1, local copies, waits for them, and re-layouts, regroup(): lax.all_to_all(values[1], 'space', split_axis=1, concat_axis=0, tiled=True)  13.2 us
    pad x2, local copies, waits for them, and re-layouts, flatten_padded(): return jnp.pad(flat, ((0, 0), (0, per_device * devices - length)))  11.7 us
  transfers between devices with their start and end apart: 3, of which 1 were waited for; matrix products, arithmetic and copies ran while one was open for 37% of the time, Pallas kernels for 0%

commit v1 on v0

--- a/solution.py
+++ b/solution.py
@@ -39,7 +39,12 @@
 def regroup(values):
     moved = (
         lax.all_to_all(
-            lax.all_to_all(values[0], "space", split_axis=1, concat_axis=0, tiled=True),
+            jnp.concatenate(
+                lax.all_to_all(
+                    jnp.stack(jnp.split(values[0], lax.axis_size("space"), axis=1)), "space", 0, 0
+                ),
+                axis=0,
+            ),
             "rec",
             split_axis=1,
             concat_axis=0,

time: 255 us -> 267 us (1.047)
  other arithmetic: 25.6 us -> 40.4 us
    unnamed x18 -> x32, local copies, waits for them, and re-layouts: 35.3 us -> 50.8 us
    another operation x0 -> x1, other arithmetic: none -> 14.1 us  [regroup(): jnp.stack(jnp.split(values[0], lax.axis_size('space'), axis=1))]
    all_to_all x0 -> x1, other arithmetic: none -> 13.5 us  [regroup(): lax.all_to_all(jnp.stack(jnp.split(values[0], lax.axis_size('space'), axi...]
    unnamed x2 -> x1, other arithmetic: 25.6 us -> 12.8 us
    all_to_all x2 -> x1, local copies, waits for them, and re-layouts: 14.6 us -> 3.02 us  [regroup(): lax.all_to_all(jnp.concatenate(lax.all_to_all(jnp.stack(jnp.split(values[...]
    pad x2 -> x1, local copies, waits for them, and re-layouts: 11.7 us -> 5.86 us  [flatten_padded(): return jnp.pad(flat, ((0, 0), (0, per_device * devices - length)))]
  transfers between devices with their start and end apart: 3 -> 3, of which waited for: 1 -> 1; matrix products, arithmetic and copies ran while one was open for 37% -> 36% of each run, Pallas kernels for 0% -> 0%
where the time goes in v1:
time: 267 us; the launch traced here: 266 us
  local copies, waits for them, and re-layouts  134 us (50%)
  blocking collectives  50.4 us (19%)
  other arithmetic  40.4 us (15%)
  starting transfers between devices  20 us (7%)
  waiting for transfers between devices  12.7 us (5%)
  matrix products  8.67 us (3%)
    unnamed x32, local copies, waits for them, and re-layouts  50.8 us
    unnamed x1, blocking collectives  45 us
    reshape x2, local copies, waits for them, and re-layouts, flatten_padded(): flat = values.reshape(receptors_here, -1)  43.2 us
    another operation x1, other arithmetic, regroup(): jnp.stack(jnp.split(values[0], lax.axis_size('space'), axis=1))  14.1 us
    all_to_all x1, other arithmetic, regroup(): lax.all_to_all(jnp.stack(jnp.split(values[0], lax.axis_size('space'), axi...  13.5 us
    all_to_all x1, local copies, waits for them, and re-layouts, regroup(): lax.all_to_all(values[1], 'space', split_axis=1, concat_axis=0, tiled=True)  13.2 us
    unnamed x1, other arithmetic  12.8 us
    all_to_all x1, waiting for transfers between devices, regroup(): lax.all_to_all(values[1], 'space', split_axis=1, concat_axis=0, tiled=True)  12.7 us
  transfers between devices with their start and end apart: 3, of which 1 were waited for; matrix products, arithmetic and copies ran while one was open for 36% of the time, Pallas kernels for 0%

profile of v1, /device:TPU:0, one launch (start us, length us, event | category | flops | bytes accessed | tf_op | source)
XLA Modules:
  0.0 266.3 jit_solution(7906830817790890155)
XLA Ops:
  0.0 5.8 %reshape.36 = bf16[8400,120]{1,0:T(8,128)(2,1)S(1)} reshape(bf16[1,120,8400]{2,1,0:T(8,128)(2,1)} %param.4) | data formatting | bytes 4032000 | tf_op jit(solution)/shard_map/reshape | solution.py:12
  5.9 2.1 convolution_convert_fusion.1
  7.9 4.1 %copy.16 = bf16[8400,120]{1,0:T(8,128)(2,1)} copy(bf16[8400,120]{0,1:T(8,128)(2,1)} %convolution_convert_fusion.1) | data formatting | bytes 4032000 | tf_op jit(solution)/shard_map/convert_element_type | solution.py:15
  12.0 2.8 %reshape.37 = bf16[120,70,120]{2,1,0:T(8,128)(2,1)S(1)} reshape(bf16[8400,120]{1,0:T(8,128)(2,1)} %copy.16) | data formatting | bytes 4032000 | tf_op jit(solution)/shard_map/reshape | solution.py:18
  14.8 2.2 convert_bitcast_fusion
  17.0 3.6 %copy.18 = bf16[120,70,120]{0,2,1:T(8,128)(2,1)S(1)} copy(bf16[120,70,120]{2,1,0:T(8,128)(2,1)} %convert_bitcast_fusion) | data formatting | bytes 4032000 | tf_op jit(solution)/shard_map/convert_element_type | solution.py:21
  20.6 2.1 fusion
  22.7 4.7 %reshape.44 = bf16[1008000]{0:T(1024)(128)(2,1)S(1)} reshape(bf16[120,8400]{1,0:T(8,128)(2,1)} %fusion) | data formatting | bytes 4032000
  27.4 23.2 %reshape.39 = bf16[1,1008000]{1,0:T(2,128)(2,1)S(1)} reshape(bf16[1008000]{0:T(1024)(128)(2,1)S(1)} %reshape.44) | data formatting | bytes 4032000 | tf_op jit(solution)/shard_map/reshape | solution.py:32
  54.4 1.0 fusion.13
  55.4 1.0 fusion.12
  58.3 1.0 fusion.9
  62.1 1.0 fusion.5
  66.5 14.1 %reduce.3 = bf16[16,63232]{1,0:T(8,128)(2,1)} reduce(bf16[16,1,63232]{2,1,0:T(2,128)(2,1)} %fusion.2, bf16[]{:T(256)} %broadcast.6), dimensions={1}, to_apply=%fusion.2.reduce_sub_computation | reduce | bytes 4046850 | tf_op jit(solution)/shard_map/stack | solution.py:44
  80.6 2.9 %reshape.48 = bf16[16,2,31616]{2,1,0:T(2,128)(2,1)} reshape(bf16[16,63232]{1,0:T(8,128)(2,1)} %reduce.3) | data formatting | bytes 4046848
  83.6 8.4 %all-to-all-start = ((bf16[16,2,31616]{2,1,0:T(2,128)(2,1)}), bf16[16,2,31616]{2,1,0:T(2,128)(2,1)}, u32[]{:S(2)}, u32[]{:S(2)}) async-start(bf16[16,2,31616]{2,1,0:T(2,128)(2,1)} %reshape.48), calls=%async_computation | async-start | bytes 4046848 | tf_op jit(solution)/shard_map/all_to_all | solution.py:43
  92.0 5.0 %reshape.46 = bf16[1008000]{0:T(1024)(128)(2,1)} reshape(bf16[1,120,8400]{2,1,0:T(8,128)(2,1)S(1)} %copy-done.2) | data formatting | bytes 4032000
  96.9 20.0 %reshape.40 = bf16[1,1008000]{1,0:T(2,128)(2,1)S(1)} reshape(bf16[1008000]{0:T(1024)(128)(2,1)} %reshape.46) | data formatting | bytes 4032000 | tf_op jit(solution)/shard_map/reshape | solution.py:32
  116.9 5.9 %pad.8 = bf16[1,1011712]{1,0:T(2,128)(2,1)} pad(bf16[1,1008000]{1,0:T(2,128)(2,1)S(1)} %reshape.40, bf16[]{:T(256)} %constant.2.clone.1), padding=0_0x0_3712 | pad | bytes 4039426 | tf_op jit(solution)/shard_map/jit(_pad)/pad | solution.py:36
  122.8 12.8 %reduce.4 = bf16[16,63232]{1,0:T(8,128)(2,1)S(1)} reduce(bf16[16,1,63232]{2,1,0:T(2,128)(2,1)} %bitcast.97, bf16[]{:T(256)} %broadcast.6), dimensions={1}, to_apply=%bitcast.85.reduce_sub_computation | reduce | bytes 4046850
  135.6 1.6 reshape.50
  137.2 6.8 %all-to-all-start.2 = ((bf16[16,2,31616]{2,1,0:T(2,128)(2,1)}), bf16[16,2,31616]{2,1,0:T(2,128)(2,1)S(1)}, u32[]{:S(2)}, u32[]{:S(2)}) async-start(bf16[16,2,31616]{2,1,0:T(2,128)(2,1)} %reshape.50), calls=%async_computation.2 | async-start | bytes 4046848 | tf_op jit(solution)/shard_map/all_to_all | solution.py:54
  144.1 12.4 %reshape.49 = bf16[16,1,63232]{2,1,0:T(2,128)(2,1)} reshape(bf16[16,2,31616]{2,1,0:T(2,128)(2,1)} %all-to-all-done) | data formatting | bytes 4046848
  156.5 13.5 %reduce = bf16[16,63232]{1,0:T(8,128)(2,1)} reduce(bf16[16,1,63232]{2,1,0:T(2,128)(2,1)} %reshape.49, bf16[]{:T(256)} %constant.11), dimensions={1}, to_apply=%all_to_all.41.reduce_sub_computation | reduce | bytes 4046850 | tf_op jit(solution)/shard_map/all_to_all | solution.py:43
  169.9 3.0 %copy.28 = bf16[2,2,8,31616]{3,2,0,1:T(8,128)(2,1)} copy(bf16[2,2,8,31616]{3,2,1,0:T(8,128)(2,1)} %bitcast.99) | data formatting | bytes 4046848 | tf_op jit(solution)/shard_map/all_to_all | solution.py:41
  172.9 12.7 %all-to-all-done.2 = bf16[16,2,31616]{2,1,0:T(2,128)(2,1)S(1)} async-done(((bf16[16,2,31616]{2,1,0:T(2,128)(2,1)}), bf16[16,2,31616]{2,1,0:T(2,128)(2,1)S(1)}, u32[]{:S(2)}, u32[]{:S(2)}) %all-to-all-start.2) | async-done | bytes 2023456 | tf_op jit(solution)/shard_map/all_to_all | solution.py:54
  185.6 4.8 %all-to-all-start.1 = ((bf16[16,2,31616]{2,0,1:T(8,128)(2,1)}), bf16[16,2,31616]{2,0,1:T(8,128)(2,1)}, u32[]{:S(2)}, u32[]{:S(2)}) async-start(bf16[16,2,31616]{2,0,1:T(8,128)(2,1)} %bitcast.101), calls=%async_computation.1 | async-start | bytes 4046848 | tf_op jit(solution)/shard_map/all_to_all | solution.py:41
  190.4 9.3 %reshape.51 = bf16[16,1,63232]{2,1,0:T(2,128)(2,1)} reshape(bf16[16,2,31616]{2,1,0:T(2,128)(2,1)S(1)} %all-to-all-done.2) | data formatting | bytes 4046848
  199.7 13.2 %bitcast_reduce_fusion = bf16[16,63232]{1,0:T(8,128)(2,1)S(1)} fusion(bf16[16,1,63232]{2,1,0:T(2,128)(2,1)} %reshape.51), kind=kLoop, calls=%fused_computation.41 | loop fusion | bytes 4046848 | tf_op jit(solution)/shard_map/all_to_all | solution.py:54
  213.0 5.4 %all_to_all.56 = bf16[16,2,31616]{2,0,1:T(8,128)(2,1)S(1)} all-to-all(bf16[16,2,31616]{2,0,1:T(8,128)(2,1)S(1)} %bitcast.102), channel_id=1, replica_groups=mesh['rec'=2,'space'=16] {'rec'}, dimensions={1} | all-to-all | bytes 4046848 | tf_op jit(solution)/shard_map/all_to_all | solution.py:53
  218.4 2.3 fusion.19
  220.7 45.0 %all-reduce.2 = f32[32,32]{1,0:T(8,128)S(1)} all-reduce(f32[32,32]{1,0:T(8,128)S(1)} %fusion.19), channel_id=2, replica_groups=mesh['rec'=2,'space'=16] {'rec','space'}, use_global_device_ids=true, to_apply=%region_0.1.clone | all-reduce | flops 1024 | bytes 8192
  (27 shorter events, 12.7 us)
Async XLA Ops:
  0.0 5.8 %copy-start = (bf16[120,120]{1,0:T(8,128)(2,1)S(1)}, bf16[120,120]{1,0:T(8,128)(2,1)}, u32[]{:S(2)}) copy-start(bf16[120,120]{1,0:T(8,128)(2,1)} %param.7) | copy-start | bytes 86404
  7.9 6.9 %copy-start.4 = (bf16[70,70]{1,0:T(8,128)(2,1)S(1)}, bf16[70,70]{1,0:T(8,128)(2,1)}, u32[]{:S(2)}) copy-start(bf16[70,70]{1,0:T(8,128)(2,1)} %param.6) | copy-start | bytes 29404
  14.8 5.8 %copy-start.3 = (bf16[120,120]{1,0:T(8,128)(2,1)S(1)}, bf16[120,120]{1,0:T(8,128)(2,1)}, u32[]{:S(2)}) copy-start(bf16[120,120]{1,0:T(8,128)(2,1)} %param.5) | copy-start | bytes 86404
  80.6 11.3 %copy-start.2 = (bf16[1,120,8400]{2,1,0:T(8,128)(2,1)S(1)}, bf16[1,120,8400]{2,1,0:T(8,128)(2,1)}, u32[]{:S(2)}) copy-start(bf16[1,120,8400]{2,1,0:T(8,128)(2,1)} %param.4) | copy-start | bytes 6048004
  83.6 53.7 %all-to-all-start = ((bf16[16,2,31616]{2,1,0:T(2,128)(2,1)}), bf16[16,2,31616]{2,1,0:T(2,128)(2,1)}, u32[]{:S(2)}, u32[]{:S(2)}) async-start(bf16[16,2,31616]{2,1,0:T(2,128)(2,1)} %reshape.48), calls=%async_computation | async-start | bytes 4046848 | tf_op jit(solution)/shard_map/all_to_all | solution.py:43
  137.2 48.4 %all-to-all-start.2 = ((bf16[16,2,31616]{2,1,0:T(2,128)(2,1)}), bf16[16,2,31616]{2,1,0:T(2,128)(2,1)S(1)}, u32[]{:S(2)}, u32[]{:S(2)}) async-start(bf16[16,2,31616]{2,1,0:T(2,128)(2,1)} %reshape.50), calls=%async_computation.2 | async-start | bytes 4046848 | tf_op jit(solution)/shard_map/all_to_all | solution.py:54
  185.6 27.4 %all-to-all-start.1 = ((bf16[16,2,31616]{2,0,1:T(8,128)(2,1)}), bf16[16,2,31616]{2,0,1:T(8,128)(2,1)}, u32[]{:S(2)}, u32[]{:S(2)}) async-start(bf16[16,2,31616]{2,0,1:T(8,128)(2,1)} %bitcast.101), calls=%async_computation.1 | async-start | bytes 4046848 | tf_op jit(solution)/shard_map/all_to_all | solution.py:41
  213.0 53.3 %copy-start.1 = (bf16[120,120]{1,0:T(8,128)(2,1)S(1)}, bf16[120,120]{1,0:T(8,128)(2,1)}, u32[]{:S(2)}) copy-start(bf16[120,120]{1,0:T(8,128)(2,1)} %param.7) | copy-start | bytes 86404
